TPU v7x, 256 devices: a whole 4x4x8 slice. The times are simulated.
256 devices in a mesh: prow: 16 (over z, core), pcol: 16 (over y, x).
Axes of the slice: x: 4, y: 4, z: 8, core: 2. Of those that a mesh axis runs over, the one named last changes fastest.
Arguments:
- kernel: float32 [3, 16, 256, 3, 16, 256], P(None, 'prow', None, None, 'pcol'), as said below
Outputs:
- factored: float32 [3, 16, 256, 3, 16, 256], P(None, 'prow', None, None, 'pcol')
Inputs may be any that keep to these rules, and one draw needn't show every extreme that they name: kernel is symmetric (entry (a, b) equals entry (b, a)); every diagonal entry is 1.1, every off-diagonal entry lies in (0, 1], and the matrix is positive definite with smallest eigenvalue at least 0.1.
All inputs are finite; a program needn't handle non-finite values.
Results may differ from a plain program's by a relative error of at most 0.0003.
Values sent between devices are 32-bit elements; how exact they have to be, the bound alone decides.
No kernel may reach another device: no remote copies, remote signals or barrier semaphores. Data moves between devices by JAX's collectives and lax.ppermute only.
A program may use at most 64 MiB of HBM per device.

v0:
```python
import jax
import jax.numpy as jnp
from jax import lax
from jax.sharding import PartitionSpec as P

HIGH = lax.Precision.HIGHEST


def chol_and_inverse(block, eye):
    lower = jnp.linalg.cholesky(block)
    inverse = jax.scipy.linalg.solve_triangular(lower, eye, lower=True)
    return (lower, inverse)


def on_device(kernel):
    prow = lax.axis_index("prow")
    pcol = lax.axis_index("pcol")
    rows = lax.axis_size("prow")
    cols = lax.axis_size("pcol")
    lbr, blk, lbc = (kernel.shape[0], kernel.shape[2], kernel.shape[3])
    work = kernel.reshape(lbr, blk, lbc, blk)
    eye = jnp.eye(blk, dtype=jnp.float32)
    zero = jnp.zeros((blk, blk), jnp.float32)
    corner_blk = work[0, :, 0, :]
    slots = jnp.stack(
        [
            jnp.where((prow == 0) & (pcol == 0), corner_blk, zero),
            jnp.where((prow == 1) & (pcol == 0), corner_blk, zero),
            jnp.where((prow == 1) & (pcol == 1), corner_blk, zero),
        ]
    )
    corner = lax.psum(slots, ("prow", "pcol"))
    own_col = work[:, :, 0, :]
    row_slots = jnp.stack([jnp.where(pcol == 0, own_col, 0.0), jnp.where(pcol == 1, own_col, 0.0)])
    row_panel = lax.psum(row_slots, "pcol")
    own_row = work[0]
    col_slots = jnp.stack([jnp.where(prow == 0, own_row, 0.0), jnp.where(prow == 1, own_row, 0.0)])
    col_panel = lax.psum(col_slots, "prow")
    l0, w0 = chol_and_inverse(corner[0], eye)
    p10 = jnp.dot(corner[1], w0.T, precision=HIGH)
    s11 = corner[2] - jnp.dot(p10, p10.T, precision=HIGH)
    l1, w1 = chol_and_inverse(s11, eye)
    r0 = jnp.einsum("aik,jk->aij", row_panel[0], w0, precision=HIGH)
    r1 = row_panel[1] - jnp.einsum("aik,jk->aij", r0, p10, precision=HIGH)
    r1 = jnp.einsum("aik,jk->aij", r1, w1, precision=HIGH)
    c0t = jnp.einsum("ik,kbj->bij", w0, col_panel[0], precision=HIGH)
    c1t = jnp.transpose(col_panel[1], (1, 0, 2)) - jnp.einsum(
        "ik,bkj->bij", p10, c0t, precision=HIGH
    )
    c1t = jnp.einsum("ik,bkj->bij", w1, c1t, precision=HIGH)
    left = jnp.concatenate([r0, r1], axis=2)
    right = jnp.concatenate([c0t, c1t], axis=1)
    trailing = work - jnp.einsum("aik,bkj->aibj", left, right, precision=HIGH)
    row_ids = jnp.arange(lbr, dtype=jnp.int32) * rows + prow
    col_ids = jnp.arange(lbc, dtype=jnp.int32) * cols + pcol
    ri = row_ids[:, None, None, None]
    cj = col_ids[None, None, :, None]
    rk = row_ids[:, None, None]
    col0 = jnp.where(rk == 0, l0[None], r0)[:, :, None, :]
    col1 = jnp.where(rk == 0, 0.0, jnp.where(rk == 1, l1[None], r1))[:, :, None, :]
    out = jnp.where(cj == 0, col0, jnp.where(cj == 1, col1, trailing))
    out = jnp.where((ri < 2) & (cj > ri), 0.0, out)
    return out.reshape(kernel.shape)


def solution(mesh):
    spec = P(None, "prow", None, None, "pcol", None)
    return jax.shard_map(on_device, mesh=mesh, in_specs=(spec,), out_specs=spec, check_vma=False)
```

profile of v0, /device:TPU:2, one launch (start us, length us, event | category | flops | bytes accessed | tf_op | source)
XLA Modules:
  0.0 512.3 jit_solution(17465115443136146933)
XLA Ops:
  6.5 5.5 %copy.2 = f32[3,1,256,3,1,256]{2,5,3,0,4,1:T(8,128)S(1)} copy(f32[3,1,256,3,1,256]{5,4,3,2,1,0:T(1,128)} %param.4) | data formatting | bytes 4718592 | tf_op args[0]
  13.1 1.1 slice-done
  14.3 1.3 pad_maximum_fusion.1
  15.8 1.2 pad_maximum_fusion
  17.7 252.8 %all-reduce.5.cloned.1.call-done = f32[3,256,256]{1,2,0:T(8,128)} async-done(((f32[3,256,256]{1,2,0:T(8,128)}), f32[3,256,256]{1,2,0:T(8,128)}) %all-reduce.5.cloned.1.call-update) | async-done | bytes 786448 | tf_op jit(solution)/shard_map/psum | solution.py:32
  272.7 11.7 %cholesky.130 = f32[128,128]{1,0:T(8,128)S(1)} custom-call(f32[128,128]{1,0:T(8,128)S(1)} %cholesky.194), custom_call_target="Cholesky" | custom-call | tf_op jit(solution)/shard_map/jit(cholesky)/cholesky | solution.py:10
  284.4 9.8 %custom-call.13 = f32[1,128,128]{1,2,0:T(8,128)S(1)} custom-call(f32[1,128,128]{2,1,0:T(8,128)S(1)} %get-tuple-element.59), custom_call_target="InvertDiagBlocksLowerTriangular" | custom-call | tf_op jit(solution)/shard_map/jit(cholesky)/cholesky | solution.py:10
  294.7 11.7 %cholesky.147 = f32[128,128]{1,0:T(8,128)S(1)} custom-call(f32[128,128]{1,0:T(8,128)S(1)} %convolution_subtract_fusion.5), custom_call_target="Cholesky" | custom-call | tf_op jit(solution)/shard_map/jit(cholesky)/cholesky | solution.py:10
  309.4 3.9 while.4
  310.0 1.3 bitcast_dynamic-update-slice_fusion.4
  312.0 1.3 bitcast_dynamic-update-slice_fusion.4
  313.3 19.8 %custom-call.14 = f32[2,128,128]{1,2,0:T(8,128)S(1)} custom-call(f32[2,128,128]{2,1,0:T(8,128)S(1)} %get-tuple-element.21), custom_call_target="InvertDiagBlocksLowerTriangular" | custom-call | tf_op jit(solution)/shard_map/jit(_solve_triangular)/triangular_solve | solution.py:11
  334.7 1.5 fusion.8
  336.3 1.4 convolution_subtract_fusion.1
  338.6 11.7 %cholesky.164 = f32[128,128]{1,0:T(8,128)S(1)} custom-call(f32[128,128]{1,0:T(8,128)S(1)} %cholesky.197), custom_call_target="Cholesky" | custom-call | tf_op jit(solution)/shard_map/jit(cholesky)/cholesky | solution.py:10
  350.3 9.8 %custom-call.15 = f32[1,128,128]{1,2,0:T(8,128)S(1)} custom-call(f32[1,128,128]{2,1,0:T(8,128)S(1)} %get-tuple-element.55), custom_call_target="InvertDiagBlocksLowerTriangular" | custom-call | tf_op jit(solution)/shard_map/jit(cholesky)/cholesky | solution.py:10
  361.2 1.1 convolution_subtract_fusion.4
  362.3 11.7 %cholesky.181 = f32[128,128]{1,0:T(8,128)S(1)} custom-call(f32[128,128]{1,0:T(8,128)S(1)} %convolution_subtract_fusion.4), custom_call_target="Cholesky" | custom-call | tf_op jit(solution)/shard_map/jit(cholesky)/cholesky | solution.py:10
  376.7 1.7 fusion.15
  378.4 3.9 while.5
  379.2 1.2 bitcast_dynamic-update-slice_fusion.5
  381.1 1.2 bitcast_dynamic-update-slice_fusion.5
  382.3 19.7 %custom-call.16 = f32[2,128,128]{1,2,0:T(8,128)S(1)} custom-call(f32[2,128,128]{2,1,0:T(8,128)S(1)} %get-tuple-element.22), custom_call_target="InvertDiagBlocksLowerTriangular" | custom-call | tf_op jit(solution)/shard_map/jit(_solve_triangular)/triangular_solve | solution.py:11
  402.0 1.8 copy.10
  403.9 1.8 copy.4
  406.3 1.8 fusion.24
  408.1 2.1 convolution_bitcast_fusion.2
  411.2 1.7 convolution_bitcast_fusion
  412.9 75.2 %all-reduce.7.cloned.1.call-done = f32[2,3,256,256]{2,3,1,0:T(8,128)} async-done(((f32[2,3,256,256]{2,3,1,0:T(8,128)}), f32[2,3,256,256]{2,3,1,0:T(8,128)}) %all-reduce.7.cloned.1.call-update) | async-done | bytes 1572880 | tf_op jit(solution)/shard_map/psum | solution.py:35
  488.1 2.1 fusion.5
  492.6 6.2 %select_bitcast_fusion = f32[3,1,256,3,1,256]{2,5,3,0,4,1:T(8,128)} fusion(f32[3,256,256]{1,2,0:T(8,128)S(1)} %get-tuple-element.66, f32[3,256,256]{1,2,0:T(8,128)S(1)} %fusion.5, f32[3,256,256]{2,1,0:T(8,128)S(1)} %copy-done, f32[3,256,256]{2,1,0:T(8,128)S(1)} %convolution_bitcast_fusion.2, f32[3,256,256]{1,2,0:T(8,128)S(1)} %get-tuple-element.61, ...), kind=kOutput, calls=%fused_computation.4 | convolution fusion | flops 3627024384 | bytes 9437199 | tf_op jit(solution)/shard_map/aik,bkj->aibj/dot_general | solution.py:53
  498.8 6.6 %copy.15 = f32[3,1,256,3,1,256]{5,4,3,2,1,0:T(1,128)} copy(f32[3,1,256,3,1,256]{2,5,3,0,4,1:T(8,128)} %select_bitcast_fusion) | data formatting | bytes 4718592 | tf_op jit(solution)/shard_map/reshape | solution.py:63
  (93 shorter events, 17.4 us)
Async XLA Ops:
  6.5 264.0 %all-reduce.5.cloned.1.call-start = ((), (), s32[]{:S(2)}) async-start(), calls=%async_computation | async-start | bytes 1572864 | tf_op jit(solution)/shard_map/psum | solution.py:32
  13.0 1.1 slice-start
  13.1 395.0 %all-reduce.9.cloned.1.call-start = ((), (), s32[]{:S(2)}) async-start(), calls=%async_computation.2 | async-start | bytes 3145728 | tf_op jit(solution)/shard_map/psum | solution.py:38
  15.6 472.5 %all-reduce.7.cloned.1.call-start = ((), (), s32[]{:S(2)}) async-start(), calls=%async_computation.1 | async-start | bytes 3145728 | tf_op jit(solution)/shard_map/psum | solution.py:35
  313.3 19.9 %copy-start.15 = (s32[2,2]{1,0:T(2,128)}, s32[2,2]{1,0:T(2,128)S(1)}, u32[]{:S(2)}) copy-start(s32[2,2]{1,0:T(2,128)S(1)} %get-tuple-element.177) | copy-start | bytes 52
  334.1 0.7 copy-start.1
  337.8 0.7 copy-start.12
  338.6 39.8 %copy-start.16 = (s32[2,2]{1,0:T(2,128)S(1)}, s32[2,2]{1,0:T(2,128)}, u32[]{:S(2)}) copy-start(s32[2,2]{1,0:T(2,128)} %copy-done.15) | copy-start | bytes 52
  374.1 2.6 copy-start.11
  402.0 3.7 copy-start.13
  406.0 2.1 copy-start.2
  408.1 2.1 copy-start.5
  410.2 0.9 copy-start.3
  410.2 1.0 copy-start.7
  488.1 2.1 copy-start.6
  490.3 0.9 copy-start.4
  490.3 1.0 copy-start.8
  490.3 1.1 copy-start.9
  490.3 1.1 copy-start.10
  490.3 1.1 copy-start.14
  491.4 1.1 copy-start
Sparse Core Ops, SparseCore 0:
  13.2 257.3 all-reduce.4
  273.0 113.0 all-reduce.8
  389.4 98.6 all-reduce.6
where the time goes:
time: 523 us; the launch traced here: 512 us
  waiting for transfers between devices  328 us (63%)
  other arithmetic  116 us (22%)
  local copies, waits for them, and re-layouts  27.6 us (5%)
  matrix products  23.7 us (5%)
  between operations  16.5 us (3%)
    psum x1, waiting for transfers between devices, on_device(): corner = lax.psum(slots, ('prow', 'pcol'))  253 us
    psum x1, waiting for transfers between devices, on_device(): row_panel = lax.psum(row_slots, 'pcol')  75.2 us
    another operation x13, other arithmetic, chol_and_inverse(): lower = jnp.linalg.cholesky(block)  68.7 us
    another operation x5, other arithmetic, chol_and_inverse(): inverse = jax.scipy.linalg.solve_triangular(lower, eye, lower=True)  42 us
  transfers between devices with their start and end apart: 3, of which 2 were waited for; matrix products, arithmetic and copies ran while one was open for 28% of the time, Pallas kernels for 0%

commit v1 on v0

--- a/solution.py
+++ b/solution.py
@@ -32,7 +32,8 @@
     corner = lax.psum(slots, ("prow", "pcol"))
     own_col = work[:, :, 0, :]
     row_slots = jnp.stack([jnp.where(pcol == 0, own_col, 0.0), jnp.where(pcol == 1, own_col, 0.0)])
-    row_panel = lax.psum(row_slots, "pcol")
+    shards = lax.all_gather(row_slots, "pcol", axis=0, tiled=False)
+    row_panel = shards.sum(axis=0)
     own_row = work[0]
     col_slots = jnp.stack([jnp.where(prow == 0, own_row, 0.0), jnp.where(prow == 1, own_row, 0.0)])
     col_panel = lax.psum(col_slots, "prow")

time: 523 us -> 552 us (1.055)
  other arithmetic: 116 us -> 130 us
  local copies, waits for them, and re-layouts: 27.6 us -> 36.4 us
    psum x1, waiting for transfers between devices: 253 us -> 331 us  [on_device(): corner = lax.psum(slots, ('prow', 'pcol'))]
    psum x1 -> x0, waiting for transfers between devices: 75.2 us -> none  [on_device(): row_panel = lax.psum(row_slots, 'pcol')]
    reduce_sum x0 -> x1, other arithmetic: none -> 10.5 us  [on_device(): row_panel = shards.sum(axis=0)]
  transfers between devices with their start and end apart: 3 -> 3, of which waited for: 2 -> 1; matrix products, arithmetic and copies ran while one was open for 28% -> 28% of each run, Pallas kernels for 0% -> 0%
where the time goes in v1:
time: 552 us; the launch traced here: 541 us
  waiting for transfers between devices  331 us (60%)
  other arithmetic  130 us (24%)
  local copies, waits for them, and re-layouts  36.4 us (7%)
  matrix products  25.9 us (5%)
  between operations  18.3 us (3%)
    psum x1, waiting for transfers between devices, on_device(): corner = lax.psum(slots, ('prow', 'pcol'))  331 us
    another operation x13, other arithmetic, chol_and_inverse(): lower = jnp.linalg.cholesky(block)  70.6 us
    another operation x5, other arithmetic, chol_and_inverse(): inverse = jax.scipy.linalg.solve_triangular(lower, eye, lower=True)  42.1 us
  transfers between devices with their start and end apart: 3, of which 1 were waited for; matrix products, arithmetic and copies ran while one was open for 28% of the time, Pallas kernels for 0%

profile of v1, /device:TPU:2, one launch (start us, length us, event | category | flops | bytes accessed | tf_op | source)
XLA Modules:
  0.0 541.1 jit_solution(14877009718348884626)
XLA Ops:
  7.4 5.5 %copy.14 = f32[3,1,256,3,1,256]{2,5,3,0,4,1:T(8,128)S(1)} copy(f32[3,1,256,3,1,256]{5,4,3,2,1,0:T(1,128)} %param.4) | data formatting | bytes 4718592 | tf_op args[0]
  15.1 1.3 pad_maximum_fusion.1
  18.0 3.1 copy.19
  21.8 330.7 %all-reduce.4.cloned.1.call-done = f32[3,256,256]{1,2,0:T(8,128)} async-done(((f32[3,256,256]{1,2,0:T(8,128)}), f32[3,256,256]{1,2,0:T(8,128)}) %all-reduce.4.cloned.1.call-update) | async-done | bytes 786448 | tf_op jit(solution)/shard_map/psum | solution.py:32
  354.6 11.7 %cholesky.130 = f32[128,128]{1,0:T(8,128)S(1)} custom-call(f32[128,128]{1,0:T(8,128)S(1)} %cholesky.194), custom_call_target="Cholesky" | custom-call | tf_op jit(solution)/shard_map/jit(cholesky)/cholesky | solution.py:10
  366.4 9.8 %custom-call.13 = f32[1,128,128]{1,2,0:T(8,128)S(1)} custom-call(f32[1,128,128]{2,1,0:T(8,128)S(1)} %get-tuple-element.59), custom_call_target="InvertDiagBlocksLowerTriangular" | custom-call | tf_op jit(solution)/shard_map/jit(cholesky)/cholesky | solution.py:10
  376.6 11.7 %cholesky.147 = f32[128,128]{1,0:T(8,128)S(1)} custom-call(f32[128,128]{1,0:T(8,128)S(1)} %convolution_subtract_fusion.5), custom_call_target="Cholesky" | custom-call | tf_op jit(solution)/shard_map/jit(cholesky)/cholesky | solution.py:10
  390.5 4.1 while.4
  391.2 1.4 bitcast_dynamic-update-slice_fusion.4
  393.3 1.4 bitcast_dynamic-update-slice_fusion.4
  395.3 19.8 %custom-call.14 = f32[2,128,128]{1,2,0:T(8,128)S(1)} custom-call(f32[2,128,128]{2,1,0:T(8,128)S(1)} %get-tuple-element.21), custom_call_target="InvertDiagBlocksLowerTriangular" | custom-call | tf_op jit(solution)/shard_map/jit(_solve_triangular)/triangular_solve | solution.py:11
  416.8 1.6 fusion.8
  418.4 1.4 convolution_subtract_fusion.1
  422.4 11.7 %cholesky.164 = f32[128,128]{1,0:T(8,128)S(1)} custom-call(f32[128,128]{1,0:T(8,128)S(1)} %cholesky.197), custom_call_target="Cholesky" | custom-call | tf_op jit(solution)/shard_map/jit(cholesky)/cholesky | solution.py:10
  434.7 10.4 %custom-call.15 = f32[1,128,128]{1,2,0:T(8,128)} custom-call(f32[1,128,128]{2,1,0:T(8,128)S(1)} %get-tuple-element.55), custom_call_target="InvertDiagBlocksLowerTriangular" | custom-call | tf_op jit(solution)/shard_map/jit(cholesky)/cholesky | solution.py:10
  447.3 11.7 %cholesky.181 = f32[128,128]{1,0:T(8,128)S(1)} custom-call(f32[128,128]{1,0:T(8,128)S(1)} %convolution_subtract_fusion.4), custom_call_target="Cholesky" | custom-call | tf_op jit(solution)/shard_map/jit(cholesky)/cholesky | solution.py:10
  459.0 1.4 compare_reduce_fusion.1
  462.5 1.9 fusion.15
  464.4 1.8 copy.24
  466.2 5.4 %while.5 = (s32[]{:T(128)}, f32[256,256]{1,0:T(8,128)S(1)}, s32[2,2]{1,0:T(2,128)}, f32[2,128,128]{2,1,0:T(8,128)S(1)}, s32[]{:T(128)}) while((s32[]{:T(128)}, f32[256,256]{1,0:T(8,128)S(1)}, s32[2,2]{1,0:T(2,128)}, f32[2,128,128]{2,1,0:T(8,128)S(1)}, s32[]{:T(128)}) %tuple.65), condition=%wide.while_cond.clone, body=%wide.while_body.clone.sunk | while | flops 2 | bytes 131189 | solution.py:11
  467.5 1.4 bitcast_dynamic-update-slice_fusion.5
  470.2 1.4 bitcast_dynamic-update-slice_fusion.5
  471.6 20.3 %custom-call.16 = f32[2,128,128]{1,2,0:T(8,128)} custom-call(f32[2,128,128]{2,1,0:T(8,128)S(1)} %get-tuple-element.22), custom_call_target="InvertDiagBlocksLowerTriangular" | custom-call | tf_op jit(solution)/shard_map/jit(_solve_triangular)/triangular_solve | solution.py:11
  493.4 1.8 fusion.24
  495.2 2.1 convolution_bitcast_fusion.2
  499.2 1.8 convolution_bitcast_fusion
  500.9 10.5 %reduce_sum.9 = f32[2,3,256,256]{3,2,1,0:T(8,128)} reduce(f32[16,2,3,256,256]{4,3,2,1,0:T(8,128)} %bitcast.153, f32[]{:T(128)} %constant.77.clone.1), dimensions={0}, to_apply=%region_5.7 | reduce | flops 5898240 | bytes 26738692 | tf_op jit(solution)/shard_map/reduce_sum | solution.py:36
  511.4 2.1 fusion.5
  514.4 2.3 copy.40
  516.8 2.1 convolution_subtract_fusion
  520.3 6.3 %select_bitcast_fusion = f32[3,1,256,3,1,256]{2,5,3,0,4,1:T(8,128)} fusion(f32[3,256,256]{1,2,0:T(8,128)S(1)} %get-tuple-element.66, f32[3,256,256]{1,2,0:T(8,128)S(1)} %fusion.5, f32[3,256,256]{2,1,0:T(8,128)S(1)} %copy-done.3, f32[3,256,256]{2,1,0:T(8,128)S(1)} %copy-done.1, f32[3,256,256]{1,2,0:T(8,128)S(1)} %get-tuple-element.61, ...), kind=kOutput, calls=%fused_computation.4 | convolution fusion | flops 3627024384 | bytes 9437199 | tf_op jit(solution)/shard_map/aik,bkj->aibj/dot_general | solution.py:54
  526.6 6.6 %copy.29 = f32[3,1,256,3,1,256]{5,4,3,2,1,0:T(1,128)} copy(f32[3,1,256,3,1,256]{2,5,3,0,4,1:T(8,128)} %select_bitcast_fusion) | data formatting | bytes 4718592 | tf_op jit(solution)/shard_map/reshape | solution.py:64
  (97 shorter events, 25.7 us)
Async XLA Ops:
  7.4 345.1 %all-reduce.4.cloned.1.call-start = ((), (), s32[]{:S(2)}) async-start(), calls=%async_computation | async-start | bytes 1572864 | tf_op jit(solution)/shard_map/psum | solution.py:32
  13.9 1.1 slice-start
  13.9 481.3 %all-reduce.6.cloned.1.call-start = ((), (), s32[]{:S(2)}) async-start(), calls=%async_computation.1 | async-start | bytes 3145728 | tf_op jit(solution)/shard_map/psum | solution.py:39
  16.5 484.4 %all-gather.3.cloned.1.call-start = ((), (), s32[]{:S(2)}) async-start(), calls=%async_computation.2 | async-start | bytes 26738688 | tf_op jit(solution)/shard_map/all_gather | solution.py:35
  394.7 0.6 copy-start.16
  416.8 78.3 %copy-start.4 = (f32[128,256]{1,0:T(8,128)}, f32[128,256]{1,0:T(8,128)S(1)}, u32[]{:S(2)}) copy-start(f32[128,256]{1,0:T(8,128)S(1)} %fusion.28) | copy-start | bytes 393220
  421.6 0.7 copy-start.14
  460.4 2.0 copy-start.13
  493.1 2.1 copy-start.5
  495.2 3.0 copy-start.8
  497.3 0.9 copy-start
  498.2 0.9 copy-start.6
  498.2 1.0 copy-start.9
  511.4 2.1 copy-start.2
  516.7 2.1 copy-start.7
  516.7 2.1 copy-start.10
  516.8 2.1 copy-start.11
  516.8 2.1 copy-start.12
  516.8 2.1 copy-start.15
  518.9 1.1 copy-start.1
  518.9 1.4 copy-start.3
Sparse Core Ops, SparseCore 0:
  14.0 338.4 all-reduce.3
  354.9 112.8 all-reduce.5
Sparse Core Ops, SparseCore 1:
  21.2 162.5 all-gather.2
